TPU v7x, 128 devices: a whole 4x4x4 slice. The times are simulated.
128 devices in a mesh: pr: 8 (over z, core), pc: 16 (over y, x).
Axes of the slice: x: 4, y: 4, z: 4, core: 2. Of those that a mesh axis runs over, the one named last changes fastest.
Arguments:
- test_points: bfloat16 [131072, 512], P('pr'), may hold values from -15 to 15
- panel_points: bfloat16 [1024, 512], P('pc'), may hold values from -15 to 15
- factor_rows: float32 [1024, 32768], P('pc', 'pr'), may hold values from -0.03125 to 0.03125
- alpha_below: float32 [32768, 128], P(('pr', 'pc')), may hold values from -6 to 6
- targets: float32 [1024, 128], P('pc'), may hold values from -6 to 6
- inverse_block: float32 [1024, 1024], P('pc'), may hold values from -0.008 to 0.08, as said below
- predictions_in: float32 [131072, 128], P(('pr', 'pc')), may hold values from -6 to 6
Outputs:
- predictions: float32 [131072, 128], P(('pr', 'pc'))
Inputs may be any that keep to these rules, and one draw needn't show every extreme that they name: `inverse_block`: lower triangular with a positive diagonal.
All inputs are finite; a program needn't handle non-finite values.
Results may differ from a plain program's by a relative error of at most 0.0003.
Values may be sent and summed in bfloat16 or wider, within the bound.
No kernel may reach another device: no remote copies, remote signals or barrier semaphores. Data moves between devices by JAX's collectives and lax.ppermute only.
A program may use at most 128 MiB of HBM per device.

v0:
```python
import math
import jax
import jax.numpy as jnp
from jax import lax
from jax.sharding import PartitionSpec as P

LAYERS = 4
bias_var = 0.1
weight_var = 2.0


def arc_kernel(panel, test, test_norms):
    width = panel.shape[1]
    cross = jnp.dot(panel, test.T, preferred_element_type=jnp.float32) / width
    panel_var = jnp.einsum("pd,pd->p", panel, panel, preferred_element_type=jnp.float32) / width
    kern = bias_var + weight_var * cross
    panel_k = bias_var + weight_var * panel_var
    test_k = bias_var + weight_var * (test_norms / width)
    for level in range(LAYERS):
        spread = jnp.sqrt(panel_k[:, None] * test_k[None, :])
        cosine = kern / spread
        theta = jnp.arccos(cosine)
        kern = bias_var + weight_var / (2.0 * math.pi) * spread * (
            jnp.sqrt(1.0 - cosine * cosine) + (math.pi - theta) * cosine
        )
        panel_k = bias_var + 0.5 * weight_var * panel_k
        test_k = bias_var + 0.5 * weight_var * test_k
    return kern


def contract_rows(left, right):
    return lax.dot_general(
        left,
        right,
        (((0,), (0,)), ((), ())),
        precision=lax.Precision.HIGHEST,
        preferred_element_type=jnp.float32,
    )


def body(
    test_points, panel_points, factor_rows, alpha_below, targets, inverse_block, predictions_in
):
    partial_sum = jnp.dot(
        factor_rows,
        lax.all_gather(alpha_below, "pc", axis=0, tiled=True),
        precision=lax.Precision.HIGHEST,
        preferred_element_type=jnp.float32,
    )
    carried = lax.psum(partial_sum, "pr")
    residual = targets - carried
    alpha_panel = lax.psum_scatter(
        contract_rows(inverse_block, residual), "pc", scatter_dimension=0, tiled=True
    )
    test_norms = jnp.einsum(
        "nd,nd->n", test_points, test_points, preferred_element_type=jnp.float32
    )
    kern = arc_kernel(panel_points, test_points, test_norms)
    update = lax.psum_scatter(
        contract_rows(kern, alpha_panel), "pc", scatter_dimension=0, tiled=True
    )
    return predictions_in + update


def solution(mesh):
    placed = (
        P("pr", None),
        P("pc", None),
        P("pc", "pr"),
        P(("pr", "pc"), None),
        P("pc", None),
        P("pc", None),
        P(("pr", "pc"), None),
    )
    return jax.shard_map(
        body, mesh=mesh, in_specs=placed, out_specs=P(("pr", "pc"), None), check_vma=False
    )
```

profile of v0, /device:TPU:0, one launch (start us, length us, event | category | flops | bytes accessed | tf_op | source)
XLA Modules:
  0.0 328.8 jit_solution(5258146334610582226)
XLA Ops:
  6.5 0.0 copy-start
  6.5 0.0 all-gather.2.cloned.1.call-start
  6.5 0.7 all-gather.2.cloned.1.call-update
  7.3 0.0 reduce-scatter.7.cloned.1.call-start
  7.3 1.0 fusion.81
  8.3 0.0 copy-start.2
  8.3 0.0 copy-start.4
  8.3 7.2 %fusion = f32[16384]{0:T(1024)S(1)} fusion(bf16[16384,512]{1,0:T(8,128)(2,1)} %param.7), kind=kLoop, calls=%fused_computation.1 | loop fusion | flops 25149440 | bytes 16842752 | tf_op jit(solution)/shard_map/nd,nd->n/dot_general | solution.py:55
  15.5 0.0 copy-start.3
  15.6 41.2 %all-gather.2.cloned.1.call-done = f32[4096,128]{1,0:T(8,128)} async-done(((f32[256,128]{1,0:T(8,128)}), f32[4096,128]{1,0:T(8,128)}) %all-gather.2.cloned.1.call-update) | async-done | bytes 2097168 | tf_op jit(solution)/shard_map/all_gather | solution.py:46
  56.7 0.0 copy-done
  56.7 3.0 fusion.87
  59.7 24.3 %psum.7 = f32[64,128]{1,0:T(8,128)S(1)} all-reduce(f32[64,128]{1,0:T(8,128)S(1)} %fusion.87), channel_id=1, replica_groups=mesh['pr'=8,'pc'=16] {'pr'}, use_global_device_ids=true, to_apply=%region_0.0 | all-reduce | flops 8192 | bytes 65536 | tf_op jit(solution)/shard_map/psum | solution.py:50
  84.0 0.0 copy-done.2
  84.0 0.0 copy-done.4
  84.0 0.6 convolution_bitcast_fusion
  84.6 1.0 copy.16
  85.6 0.0 reduce-scatter.7.cloned.1.call-update
  85.7 0.0 reduce-scatter.5.cloned.1.call-start
  85.7 0.0 copy-done.3
  85.7 12.9 %fusion.2 = f32[64,16384]{1,0:T(8,128)} fusion(bf16[64,512]{1,0:T(8,128)(2,1)S(1)} %copy-done.3, bf16[16384,512]{1,0:T(8,128)(2,1)} %param.7, f32[16384]{0:T(1024)S(1)} %get-tuple-element.8, f32[64]{0:T(128)S(1)} %get-tuple-element.12), kind=kOutput, calls=%fused_computation.4 | convolution fusion | flops 1077936128 | bytes 21102848 | tf_op jit(solution)/shard_map/dot_general | solution.py:14
  98.6 57.3 %reduce-scatter.7.cloned.1.call-done = f32[64,128]{1,0:T(8,128)} async-done(((f32[1024,128]{1,0:T(8,128)}), f32[64,128]{1,0:T(8,128)}) %reduce-scatter.7.cloned.1.call-update) | async-done | bytes 32784
  156.0 78.8 %fusion.3 = f32[16384,128]{1,0:T(8,128)} fusion(f32[64,128]{1,0:T(8,128)} %reduce-scatter.7.cloned.1.call-done, f32[64,16384]{1,0:T(8,128)} %fusion.2, f32[16384]{0:T(1024)S(1)} %get-tuple-element.8, f32[64]{0:T(128)S(1)} %get-tuple-element.12, f32[16384]{0:T(1024)S(1)} %get-tuple-element.7, f32[64]{0:T(128)S(1)} %get-tuple-element.11, ...), kind=kOutput, calls=%fused_computation.5 | convolution fusion | flops 1664090112 | bytes 12878848 | tf_op jit(solution)/shard_map/dot_general | solution.py:32
  234.8 0.0 copy-start.1
  234.8 0.0 reduce-scatter.5.cloned.1.call-update
  234.8 85.3 %reduce-scatter.5.cloned.1.call-done = f32[1024,128]{1,0:T(8,128)} async-done(((f32[16384,128]{1,0:T(8,128)}), f32[1024,128]{1,0:T(8,128)}) %reduce-scatter.5.cloned.1.call-update) | async-done | bytes 524304 | tf_op jit(solution)/shard_map/reduce_scatter | solution.py:59
  320.0 0.0 copy-done.1
  320.0 1.9 add.111
  (2 shorter events, 0.0 us)
Async XLA Ops:
  6.5 50.2 %copy-start = (f32[64,4096]{1,0:T(8,128)S(1)}, f32[64,4096]{1,0:T(8,128)}, u32[]{:S(2)}) copy-start(f32[64,4096]{1,0:T(8,128)} %param.9) | copy-start | bytes 3145732
  6.5 50.2 %all-gather.2.cloned.1.call-start = ((), (), s32[]{:S(2)}) async-start(), calls=%async_computation.2 | async-start | bytes 2228224 | tf_op jit(solution)/shard_map/all_gather | solution.py:46
  7.3 148.7 %reduce-scatter.7.cloned.1.call-start = ((), (), s32[]{:S(2)}) async-start(), calls=%async_computation.4 | async-start | bytes 557056
  8.3 75.7 %copy-start.2 = (f32[64,1024]{1,0:T(8,128)S(1)}, f32[64,1024]{1,0:T(8,128)}, u32[]{:S(2)}) copy-start(f32[64,1024]{1,0:T(8,128)} %param.12) | copy-start | bytes 786436
  8.3 75.7 %copy-start.4 = (f32[64,128]{1,0:T(8,128)S(1)}, f32[64,128]{1,0:T(8,128)}, u32[]{:S(2)}) copy-start(f32[64,128]{1,0:T(8,128)} %param.11) | copy-start | bytes 98308
  15.5 70.2 %copy-start.3 = (bf16[64,512]{1,0:T(8,128)(2,1)S(1)}, bf16[64,512]{1,0:T(8,128)(2,1)}, u32[]{:S(2)}) copy-start(bf16[64,512]{1,0:T(8,128)(2,1)} %param.8) | copy-start | bytes 196612
  85.7 234.4 %reduce-scatter.5.cloned.1.call-start = ((), (), s32[]{:S(2)}) async-start(), calls=%async_computation.3 | async-start | bytes 8912896 | tf_op jit(solution)/shard_map/reduce_scatter | solution.py:59
  234.8 85.3 %copy-start.1 = (f32[1024,128]{1,0:T(8,128)S(1)}, f32[1024,128]{1,0:T(8,128)}, u32[]{:S(2)}) copy-start(f32[1024,128]{1,0:T(8,128)} %param.13) | copy-start | bytes 1572868
Sparse Core Ops, SparseCore 0:
  9.5 47.2 all-gather.1
  85.8 70.1 reduce-scatter.6
  234.9 85.0 reduce-scatter.4
where the time goes:
time: 334 us; the launch traced here: 329 us
  waiting for transfers between devices  184 us (55%)
  matrix products  95.3 us (29%)
  blocking collectives  24.3 us (7%)
  between operations  13.6 us (4%)
  other arithmetic  10.1 us (3%)
    reduce_scatter x1, waiting for transfers between devices, body(): lax.psum_scatter(contract_rows(kern, alpha_panel), 'pc', scatter_dimensio...  85.3 us
    dot_general x2, matrix products, contract_rows(): lax.dot_general(left, right, (((0,), (0,)), ((), ())), precision=lax.Prec...  79.4 us
    unnamed x4, waiting for transfers between devices  58.1 us
    all_gather x1, waiting for transfers between devices, body(): lax.all_gather(alpha_below, 'pc', axis=0, tiled=True)  41.2 us
    psum x1, blocking collectives, body(): carried = lax.psum(partial_sum, 'pr')  24.3 us
    dot_general x1, matrix products, arc_kernel(): cross = jnp.dot(panel, test.T, preferred_element_type=jnp.float32) / width  12.9 us
    dot_general x1, other arithmetic, body(): jnp.einsum('nd,nd->n', test_points, test_points, preferred_element_type=j...  7.24 us
  transfers between devices with their start and end apart: 3, of which 3 were waited for; matrix products, arithmetic and copies ran while one was open for 6% of the time, Pallas kernels for 0%

commit v1 on v0

--- a/solution.py
+++ b/solution.py
@@ -47,7 +47,9 @@
         precision=lax.Precision.HIGHEST,
         preferred_element_type=jnp.float32,
     )
-    carried = lax.psum(partial_sum, "pr")
+    carried = partial_sum
+    for hop in (1, 2, 4):
+        carried = carried + lax.ppermute(carried, "pr", [(dev, dev ^ hop) for dev in range(8)])
     residual = targets - carried
     alpha_panel = lax.psum_scatter(
         contract_rows(inverse_block, residual), "pc", scatter_dimension=0, tiled=True

time: 334 us -> 324 us (0.970)
  blocking collectives: 24.3 us -> 0 us
  waiting for transfers between devices: 184 us -> 194 us
  starting transfers between devices: 0.08 us -> 4.87 us
    psum x1 -> x0, blocking collectives: 24.3 us -> none  [body(): carried = lax.psum(partial_sum, 'pr')]
    ppermute x0 -> x3, waiting for transfers between devices: none -> 5.67 us  [body(): lax.ppermute(carried, 'pr', [(dev, dev ^ hop) for dev in range(8)])]
    ppermute x0 -> x3, starting transfers between devices: none -> 4.79 us  [body(): lax.ppermute(carried, 'pr', [(dev, dev ^ hop) for dev in range(8)])]
  transfers between devices with their start and end apart: 3 -> 6, of which waited for: 3 -> 6; matrix products, arithmetic and copies ran while one was open for 6% -> 6% of each run, Pallas kernels for 0% -> 0%
where the time goes in v1:
time: 324 us; the launch traced here: 318 us
  waiting for transfers between devices  194 us (60%)
  matrix products  95.3 us (29%)
  between operations  13.6 us (4%)
  other arithmetic  9.27 us (3%)
  starting transfers between devices  4.87 us (2%)
    reduce_scatter x1, waiting for transfers between devices, body(): lax.psum_scatter(contract_rows(kern, alpha_panel), 'pc', scatter_dimensio...  85.3 us
    dot_general x2, matrix products, contract_rows(): lax.dot_general(left, right, (((0,), (0,)), ((), ())), precision=lax.Prec...  79.5 us
    unnamed x4, waiting for transfers between devices  60.7 us
    all_gather x1, waiting for transfers between devices, body(): lax.all_gather(alpha_below, 'pc', axis=0, tiled=True)  42.2 us
    dot_general x1, matrix products, arc_kernel(): cross = jnp.dot(panel, test.T, preferred_element_type=jnp.float32) / width  12.9 us
    dot_general x1, other arithmetic, body(): jnp.einsum('nd,nd->n', test_points, test_points, preferred_element_type=j...  7.23 us
  transfers between devices with their start and end apart: 6, of which 6 were waited for; matrix products, arithmetic and copies ran while one was open for 6% of the time, Pallas kernels for 0%

profile of v1, /device:TPU:0, one launch (start us, length us, event | category | flops | bytes accessed | tf_op | source)
XLA Modules:
  0.0 317.9 jit_solution(8048840663430292874)
XLA Ops:
  6.5 0.0 copy-start
  6.5 0.0 all-gather.2.cloned.1.call-start
  6.5 0.7 all-gather.2.cloned.1.call-update
  7.3 0.0 copy-start.3
  7.3 0.0 copy-start.2
  7.3 0.0 copy-start.4
  7.3 0.0 reduce-scatter.7.cloned.1.call-start
  7.3 7.2 %fusion = f32[16384]{0:T(1024)S(1)} fusion(bf16[16384,512]{1,0:T(8,128)(2,1)} %param.7), kind=kLoop, calls=%fused_computation.1 | loop fusion | flops 25149440 | bytes 16842752 | tf_op jit(solution)/shard_map/nd,nd->n/dot_general | solution.py:57
  14.6 42.2 %all-gather.2.cloned.1.call-done = f32[4096,128]{1,0:T(8,128)} async-done(((f32[256,128]{1,0:T(8,128)}), f32[4096,128]{1,0:T(8,128)}) %all-gather.2.cloned.1.call-update) | async-done | bytes 2097168 | tf_op jit(solution)/shard_map/all_gather | solution.py:46
  56.7 0.0 copy-done
  56.7 3.0 fusion.88
  59.7 0.1 collective-permute-start
  59.8 1.2 collective-permute-done
  61.0 1.6 collective-permute-start.1
  62.6 0.0 copy-done.3
  62.6 0.1 fusion.81
  62.7 2.2 collective-permute-done.1
  64.9 3.1 collective-permute-start.2
  68.1 2.3 collective-permute-done.2
  70.4 0.0 copy-done.2
  70.4 0.0 copy-done.4
  70.4 0.6 convolution_bitcast_fusion
  71.0 1.0 copy.16
  72.0 0.0 reduce-scatter.7.cloned.1.call-update
  72.0 0.0 reduce-scatter.5.cloned.1.call-start
  72.1 12.9 %fusion.2 = f32[64,16384]{1,0:T(8,128)} fusion(bf16[64,512]{1,0:T(8,128)(2,1)S(1)} %copy-done.3, bf16[16384,512]{1,0:T(8,128)(2,1)} %param.7, f32[16384]{0:T(1024)S(1)} %get-tuple-element.8, f32[64]{0:T(128)S(1)} %get-tuple-element.12), kind=kOutput, calls=%fused_computation.4 | convolution fusion | flops 1077936128 | bytes 21102848 | tf_op jit(solution)/shard_map/dot_general | solution.py:14
  85.0 59.9 %reduce-scatter.7.cloned.1.call-done = f32[64,128]{1,0:T(8,128)} async-done(((f32[1024,128]{1,0:T(8,128)}), f32[64,128]{1,0:T(8,128)}) %reduce-scatter.7.cloned.1.call-update) | async-done | bytes 32784
  144.9 78.8 %fusion.3 = f32[16384,128]{1,0:T(8,128)} fusion(f32[64,128]{1,0:T(8,128)} %reduce-scatter.7.cloned.1.call-done, f32[64,16384]{1,0:T(8,128)} %fusion.2, f32[16384]{0:T(1024)S(1)} %get-tuple-element.8, f32[64]{0:T(128)S(1)} %get-tuple-element.12, f32[16384]{0:T(1024)S(1)} %get-tuple-element.7, f32[64]{0:T(128)S(1)} %get-tuple-element.11, ...), kind=kOutput, calls=%fused_computation.5 | convolution fusion | flops 1664090112 | bytes 12878848 | tf_op jit(solution)/shard_map/dot_general | solution.py:32
  223.7 0.0 copy-start.1
  223.7 0.0 reduce-scatter.5.cloned.1.call-update
  223.8 85.3 %reduce-scatter.5.cloned.1.call-done = f32[1024,128]{1,0:T(8,128)} async-done(((f32[16384,128]{1,0:T(8,128)}), f32[1024,128]{1,0:T(8,128)}) %reduce-scatter.5.cloned.1.call-update) | async-done | bytes 524304 | tf_op jit(solution)/shard_map/reduce_scatter | solution.py:61
  309.1 0.0 copy-done.1
  309.1 1.9 add.121
  (4 shorter events, 0.0 us)
Async XLA Ops:
  6.5 50.2 %copy-start = (f32[64,4096]{1,0:T(8,128)S(1)}, f32[64,4096]{1,0:T(8,128)}, u32[]{:S(2)}) copy-start(f32[64,4096]{1,0:T(8,128)} %param.9) | copy-start | bytes 3145732
  6.5 50.2 %all-gather.2.cloned.1.call-start = ((), (), s32[]{:S(2)}) async-start(), calls=%async_computation.2 | async-start | bytes 2228224 | tf_op jit(solution)/shard_map/all_gather | solution.py:46
  7.3 55.3 %copy-start.3 = (bf16[64,512]{1,0:T(8,128)(2,1)S(1)}, bf16[64,512]{1,0:T(8,128)(2,1)}, u32[]{:S(2)}) copy-start(bf16[64,512]{1,0:T(8,128)(2,1)} %param.8) | copy-start | bytes 196612
  7.3 63.1 %copy-start.2 = (f32[64,1024]{1,0:T(8,128)S(1)}, f32[64,1024]{1,0:T(8,128)}, u32[]{:S(2)}) copy-start(f32[64,1024]{1,0:T(8,128)} %param.12) | copy-start | bytes 786436
  7.3 63.1 %copy-start.4 = (f32[64,128]{1,0:T(8,128)S(1)}, f32[64,128]{1,0:T(8,128)}, u32[]{:S(2)}) copy-start(f32[64,128]{1,0:T(8,128)} %param.11) | copy-start | bytes 98308
  7.3 137.6 %reduce-scatter.7.cloned.1.call-start = ((), (), s32[]{:S(2)}) async-start(), calls=%async_computation.4 | async-start | bytes 557056
  59.7 1.3 collective-permute-start
  61.0 3.9 %collective-permute-start.1 = (f32[64,128]{1,0:T(8,128)S(1)}, f32[64,128]{1,0:T(8,128)S(1)}, u32[]{:S(2)}, u32[]{:S(2)}) collective-permute-start(f32[64,128]{1,0:T(8,128)S(1)} %add.118), channel_id=1, source_target_pairs={{0,32},{16,48},{32,0},{48,16},{64,96},{80,112},{96,64},{112,80},{1... | collective-permute-start | bytes 98312 | tf_op jit(solution)/shard_map/ppermute | solution.py:52
  64.9 5.4 %collective-permute-start.2 = (f32[64,128]{1,0:T(8,128)S(1)}, f32[64,128]{1,0:T(8,128)S(1)}, u32[]{:S(2)}, u32[]{:S(2)}) collective-permute-start(f32[64,128]{1,0:T(8,128)S(1)} %add.119), channel_id=1, source_target_pairs={{0,64},{16,80},{32,96},{48,112},{64,0},{80,16},{96,32},{112,48},{1... | collective-permute-start | bytes 98312 | tf_op jit(solution)/shard_map/ppermute | solution.py:52
  72.0 237.1 %reduce-scatter.5.cloned.1.call-start = ((), (), s32[]{:S(2)}) async-start(), calls=%async_computation.3 | async-start | bytes 8912896 | tf_op jit(solution)/shard_map/reduce_scatter | solution.py:61
  223.7 85.4 %copy-start.1 = (f32[1024,128]{1,0:T(8,128)S(1)}, f32[1024,128]{1,0:T(8,128)}, u32[]{:S(2)}) copy-start(f32[1024,128]{1,0:T(8,128)} %param.13) | copy-start | bytes 1572868
Sparse Core Ops, SparseCore 0:
  9.5 47.2 all-gather.1
  72.1 72.7 reduce-scatter.6
  223.9 85.1 reduce-scatter.4
